TPU v7x, 256 devices: a whole 4x4x8 slice. The times are simulated.
256 devices in a mesh: dp: 8 (over x, z_hi), tensor: 32 (over y, z_lo, core).
Axes of the slice: x: 4, y: 4, z: 8 (z_hi: 2, z_lo: 4; z = z_hi * 4 + z_lo), core: 2. Of those that a mesh axis runs over, the one named last changes fastest.
Arguments:
- tokens: bfloat16 [8, 4096, 1280], P('dp', 'tensor'), may hold values from -6 to 6
- segment_ids: int32 [8, 4096], P('dp', 'tensor'), may hold values from 0 to 3, never falling along the last dimension, each value on 1 to 2048 neighbouring positions
- pack_of_group: int32 [32], replicated, may hold values from 0 to 31, each once
- w_qkv: bfloat16 [1280, 1920], replicated, may hold values from -0.11320094 to 0.11320094
- qk_gain: float32 [640], replicated, may hold values from 0.5 to 7
- w_out: bfloat16 [640, 1280], replicated, may hold values from -0.25 to 0.25
- alpha_attn: float32 [1280], replicated, may hold values from 0.05 to 0.6
- w_up: bfloat16 [1280, 5120], P(None, 'dp'), may hold values from -0.15625 to 0.15625
- w_gate: bfloat16 [1280, 5120], P(None, 'dp'), may hold values from -0.15625 to 0.15625
- up_gain: float32 [5120], P('dp'), may hold values from 0.5 to 2
- gate_gain: float32 [5120], P('dp'), may hold values from 0.5 to 2
- w_down: bfloat16 [5120, 1280], P('dp'), may hold values from -0.078125 to 0.078125
- alpha_mlp: float32 [1280], replicated, may hold values from 0.05 to 0.6
- w_vocab: bfloat16 [1280, 32000], P(None, ('dp', 'tensor')), may hold values from -0.15625 to 0.15625
- logit_gain: bfloat16 [32000], P(('dp', 'tensor')), may hold values from 1 to 10
Outputs:
- result_rows: bfloat16 [8, 4096, 1280], P('dp', 'tensor')
- request_norm: float32 [32], replicated
- max_logit: float32 [32], replicated
Inputs may be any that keep to these rules, and one draw needn't show every extreme that they name: `segment_ids`: within a pack the request numbers never fall, every request 0 to 3 has one or more tokens, and one request has exactly 2048 tokens.
All inputs are finite; a program needn't handle non-finite values.
Results may differ from a plain program's by a relative error of at most 0.013.
Values may be sent and summed in bfloat16 or wider, within the bound.
No kernel may reach another device: no remote copies, remote signals or barrier semaphores. Data moves between devices by JAX's collectives and lax.ppermute only.
A program may use at most 128 MiB of HBM per device.

v0:
```python
import math
import jax
import jax.numpy as jnp
from jax import lax
from jax.sharding import PartitionSpec as P

HEADS = 10
HD = 64
REQS = 4
EPSILON = 1e-06
NEGATIVE = -1e30


def normalize(values):
    return values * lax.rsqrt(jnp.mean(values * values, axis=-1, keepdims=True) + EPSILON)


def head_norm(values, qk_gain):
    reshaped = values.reshape(values.shape[0], HEADS, HD)
    return (normalize(reshaped) * qk_gain.reshape(HEADS, HD)).astype(jnp.bfloat16)


def local(
    tokens,
    segment_ids,
    pack_of_group,
    w_qkv,
    qk_gain,
    w_out,
    alpha_attn,
    w_up,
    w_gate,
    up_gain,
    gate_gain,
    w_down,
    alpha_mlp,
    w_vocab,
    logit_gain,
):
    row_count = tokens.shape[1]
    head_width = HEADS * HD
    segments = segment_ids[0]
    tensor_index = lax.axis_index("tensor")
    positions = tensor_index * row_count + jnp.arange(row_count, dtype=jnp.int32)
    request_numbers = jnp.arange(REQS, dtype=jnp.int32)
    start_rows = normalize(tokens[0].astype(jnp.float32)).astype(jnp.bfloat16)
    projected = jnp.dot(start_rows, w_qkv, preferred_element_type=jnp.float32)
    queries = head_norm(projected[:, :head_width], qk_gain)
    key_rows = head_norm(projected[:, head_width : 2 * head_width], qk_gain).reshape(
        row_count, head_width
    )
    value_rows = projected[:, 2 * head_width :].astype(jnp.bfloat16)
    score_scale = 1.0 / math.sqrt(HD)
    packed = jnp.concatenate([key_rows, value_rows], axis=1)
    gathered = lax.all_gather(packed, "tensor", axis=0, tiled=False)
    vocab_pack = jnp.concatenate(
        [w_vocab, logit_gain[None], jnp.zeros((7, w_vocab.shape[1]), w_vocab.dtype)], axis=0
    )
    vocab_pack, gathered = lax.optimization_barrier((vocab_pack, gathered))
    vocab_all = lax.all_gather(vocab_pack, "dp", axis=0, tiled=False)
    key_all = gathered[:, :row_count, :head_width].reshape(-1, head_width)
    value_all = gathered[:, :row_count, head_width:].reshape(-1, head_width)
    seg_all = lax.all_gather(segments, "tensor", axis=0, tiled=True)
    tally = jnp.sum((seg_all[:, None] == request_numbers[None, :]).astype(jnp.int32), axis=0)
    total_keys = key_all.shape[0]
    key_pos = jnp.arange(total_keys, dtype=jnp.int32)
    head_of_column = jnp.arange(head_width, dtype=jnp.int32) // HD
    head_mask = (jnp.arange(HEADS, dtype=jnp.int32)[:, None] == head_of_column[None, :]).astype(
        jnp.bfloat16
    )
    query_flat = queries.reshape(row_count, head_width)
    query_blocks = (query_flat[None, :, :] * head_mask[:, None, :]).reshape(
        HEADS * row_count, head_width
    )
    scores = (
        lax.dot_general(
            query_blocks, key_all, (((1,), (1,)), ((), ())), preferred_element_type=jnp.float32
        ).reshape(HEADS, row_count, total_keys)
        * score_scale
    )
    allowed = (seg_all[None, :] == segments[:, None]) & (key_pos[None, :] <= positions[:, None])
    row_max = jnp.max(jnp.where(allowed[None], scores, NEGATIVE), axis=2)
    weights = jnp.where(allowed[None], jnp.exp(scores - row_max[:, :, None]), 0.0)
    weight_sum = jnp.sum(weights, axis=2)
    weighted = jnp.dot(
        weights.astype(jnp.bfloat16).reshape(HEADS * row_count, total_keys),
        value_all,
        preferred_element_type=jnp.float32,
    ).reshape(HEADS, row_count, head_width)
    attended = jnp.sum(
        weighted / weight_sum[:, :, None] * head_mask[:, None, :].astype(jnp.float32), axis=0
    ).astype(jnp.bfloat16)
    attn_rows = normalize(jnp.dot(attended, w_out, preferred_element_type=jnp.float32))
    residual_in = start_rows.astype(jnp.float32)
    mid_rows = normalize(residual_in + alpha_attn * (attn_rows - residual_in)).astype(jnp.bfloat16)
    mid_rows, vocab_all = lax.optimization_barrier((mid_rows, vocab_all))
    received = lax.all_gather(mid_rows, "dp", axis=0, tiled=True)
    up_proj = jnp.dot(received, w_up, preferred_element_type=jnp.float32) * up_gain
    gate_proj = jnp.dot(received, w_gate, preferred_element_type=jnp.float32) * gate_gain
    hidden = (up_proj * jax.nn.silu(gate_proj)).astype(jnp.bfloat16)
    mixed_sum = lax.psum_scatter(
        jnp.dot(hidden, w_down, preferred_element_type=jnp.float32).astype(jnp.bfloat16),
        "dp",
        scatter_dimension=0,
        tiled=True,
    ).astype(jnp.float32)
    mlp_rows = normalize(mixed_sum)
    residual_mid = mid_rows.astype(jnp.float32)
    result_rows = normalize(residual_mid + alpha_mlp * (mlp_rows - residual_mid)).astype(
        jnp.bfloat16
    )
    request_ends = jnp.cumsum(tally) - 1
    same_request = segments[:, None] == request_numbers[None, :]
    row_end = jnp.sum(jnp.where(same_request, request_ends[None, :], 0), axis=1)
    is_last = positions == row_end
    member = same_request.astype(jnp.float32)
    chosen = member * is_last[:, None].astype(jnp.float32)
    result_f32 = result_rows.astype(jnp.float32)
    row_sums = jnp.dot(
        member.T.astype(jnp.bfloat16), result_rows, preferred_element_type=jnp.float32
    )
    last_rows = jnp.dot(
        chosen.T.astype(jnp.bfloat16), result_rows, preferred_element_type=jnp.float32
    )
    partial = jnp.concatenate([row_sums, last_rows], axis=0)
    summed = jnp.sum(
        lax.all_gather(partial.astype(jnp.bfloat16), "tensor", axis=0, tiled=False).astype(
            jnp.float32
        ),
        axis=0,
    )
    row_sums, last_rows = (summed[:REQS], summed[REQS:])
    counts = tally.astype(jnp.float32)
    request_mean = row_sums / counts[:, None]
    group_norm = jnp.sqrt(jnp.mean(request_mean * request_mean, axis=1))
    slot_count = lax.axis_size("dp") * REQS
    dp_index = lax.axis_index("dp")
    model_width = last_rows.shape[1]
    pack_logits = jnp.einsum(
        "rd,gdc->rgc",
        last_rows.astype(jnp.bfloat16),
        vocab_all[:, :model_width],
        preferred_element_type=jnp.float32,
    ) * vocab_all[None, :, model_width].astype(jnp.float32)
    pack_max = jnp.max(pack_logits.reshape(REQS, -1), axis=1)
    own_slot = jnp.arange(slot_count, dtype=jnp.int32) // REQS == dp_index
    spread_max = jnp.where(own_slot, jnp.tile(pack_max, slot_count // REQS), NEGATIVE)
    spread_norm = jnp.where(own_slot, jnp.tile(group_norm, slot_count // REQS), NEGATIVE)
    every = lax.pmax(jnp.concatenate([spread_max, spread_norm]), ("dp", "tensor"))
    every_max, every_norm = (every[:slot_count], every[slot_count:])
    placement = (pack_of_group[:, None] == jnp.arange(slot_count, dtype=jnp.int32)[None, :]).astype(
        jnp.float32
    )
    request_norm = jnp.dot(every_norm, placement, precision=lax.Precision.HIGHEST)
    max_logit = jnp.dot(every_max, placement, precision=lax.Precision.HIGHEST)
    return (result_rows[None], request_norm, max_logit)


def solution(mesh):
    return jax.shard_map(
        local,
        mesh=mesh,
        in_specs=(
            P("dp", "tensor", None),
            P("dp", "tensor"),
            P(),
            P(),
            P(),
            P(),
            P(),
            P(None, "dp"),
            P(None, "dp"),
            P("dp"),
            P("dp"),
            P("dp", None),
            P(),
            P(None, ("dp", "tensor")),
            P(("dp", "tensor")),
        ),
        out_specs=(P("dp", "tensor", None), P(), P()),
        check_vma=False,
    )
```

profile of v0, /device:TPU:1, one launch (start us, length us, event | category | flops | bytes accessed | tf_op | source)
XLA Modules:
  0.0 512.1 jit_solution(1264424142614423006)
XLA Ops:
  7.2 1.2 fusion.30
  8.5 3.4 fusion.62
  12.9 1.0 reduce_sum.118
  13.9 0.9 copy.27
  15.3 1.0 multiply_convert_fusion.4
  17.2 3.1 concatenate.24
  20.3 46.1 %all-gather = s32[1,4096]{1,0:T(1,128)S(1)} all-gather(s32[1,128]{1,0:T(1,128)S(1)} %copy-done.8), channel_id=2, replica_groups=mesh['dp'=8,'tensor'=32] {'tensor'}, dimensions={1}, use_global_device_ids=true | all-gather | bytes 16896 | tf_op jit(solution)/shard_map/all_gather | solution.py:63
  66.9 26.5 %all-gather.9.cloned.1.call-done = bf16[4096,1280]{1,0:T(8,128)(2,1)} async-done(((bf16[128,1280]{1,0:T(8,128)(2,1)}), bf16[4096,1280]{1,0:T(8,128)(2,1)}) %all-gather.9.cloned.1.call-update) | async-done | bytes 10485776 | tf_op jit(solution)/shard_map/all_gather | solution.py:55
  93.5 9.6 %fusion.64 = (bf16[32,128,640]{2,1,0:T(8,128)(2,1)}, bf16[32,128,640]{2,1,0:T(8,128)(2,1)}) fusion(bf16[32,128,1280]{2,1,0:T(8,128)(2,1)} %bitcast.58), kind=kLoop, calls=%fused_computation.115 | loop fusion | bytes 20971520 | tf_op jit(solution)/shard_map/slice | solution.py:61
  103.3 13.9 %fusion.17 = f32[10,128,4096]{2,1,0:T(8,128)} fusion(bf16[4096,640,1]{1,0,2:T(8,128)(2,1)} %bitcast.60, bf16[10,640]{1,0:T(8,128)(2,1)S(1)} %get-tuple-element.17, bf16[128,640]{1,0:T(8,128)(2,1)S(1)} %get-tuple-element.13), kind=kOutput, calls=%fused_computation.21 | convolution fusion | flops 6711705600 | bytes 26391040 | tf_op jit(solution)/shard_map/dot_general | solution.py:76
  117.3 21.3 %fusion.65 = f32[10,128]{1,0:T(8,128)S(1)} fusion(f32[10,128,4096]{2,1,0:T(8,128)} %fusion.17, pred[128,4096]{1,0:T(8,128)(4,1)S(1)} %fusion.14), kind=kOutput, calls=%fused_computation.116 | output fusion | flops 31461376 | bytes 21500928 | tf_op jit(solution)/shard_map/sub | solution.py:83
  138.6 25.4 %multiply_reduce_fusion = bf16[128,640]{1,0:T(8,128)(2,1)S(1)} fusion(bf16[4096,640,1]{1,0,2:T(8,128)(2,1)} %bitcast.59, f32[10,640]{1,0:T(8,128)S(1)} %get-tuple-element.18, f32[10,128]{1,0:T(8,128)S(1)} %fusion.65, f32[10,128,4096]{2,1,0:T(8,128)} %fusion.17, pred[128,4096]{1,0:T(8,128)(4,1)} %copy-done.5), kind=kOutput, calls=%fused_computation.11 | convolution fusion | flops 6744724480 | bytes 26933248 | tf_op jit(solution)/shard_map/dot_general | solution.py:85
  165.3 1.0 multiply_convert_fusion.2
  166.3 18.2 %all-gather.11.cloned.1.call-done = bf16[10304,125]{1,0:T(8,128)(2,1)} async-done(((bf16[1288,125]{1,0:T(8,128)(2,1)}), bf16[10304,125]{1,0:T(8,128)(2,1)}) %all-gather.11.cloned.1.call-update) | async-done | bytes 2576016 | tf_op jit(solution)/shard_map/all_gather | solution.py:60
  184.6 82.3 %all-gather.7.cloned.1.call-done = bf16[1024,1280]{1,0:T(8,128)(2,1)} async-done(((bf16[128,1280]{1,0:T(8,128)(2,1)}), bf16[1024,1280]{1,0:T(8,128)(2,1)}) %all-gather.7.cloned.1.call-update) | async-done | bytes 2621456 | tf_op jit(solution)/shard_map/all_gather | solution.py:97
  266.9 5.4 %fusion.66 = f32[1024,640]{1,0:T(8,128)} fusion(bf16[1024,1280]{1,0:T(8,128)(2,1)} %all-gather.7.cloned.1.call-done, bf16[1280,640]{1,0:T(8,128)(2,1)S(1)} %copy-done.11), kind=kOutput, calls=%fused_computation.117 | convolution fusion | flops 1677721600 | bytes 6881280 | tf_op jit(solution)/shard_map/dot_general | solution.py:98
  272.3 8.9 %convolution_convert_fusion = bf16[1024,1280]{1,0:T(8,128)(2,1)} fusion(bf16[640,1280]{1,0:T(8,128)(2,1)S(1)} %copy-done, f32[1024,640]{1,0:T(8,128)} %fusion.66, bf16[1024,1280]{1,0:T(8,128)(2,1)} %all-gather.7.cloned.1.call-done, bf16[1280,640]{1,0:T(8,128)(2,1)} %param.23, f32[640]{0:T(1024)S(1)} %copy-done.12, f32[640]{0:T(1024)S(1)} %copy-done.13), kind=kOutput, calls=%fused_computation.10 | convolution fusion | flops 3361996800 | bytes 11146240 | tf_op jit(solution)/shard_map/dot_general | solution.py:102
  282.4 95.8 %reduce-scatter.2.cloned.1.call-done = bf16[128,1280]{1,0:T(8,128)(2,1)} async-done(((bf16[1024,1280]{1,0:T(8,128)(2,1)}), bf16[128,1280]{1,0:T(8,128)(2,1)}) %reduce-scatter.2.cloned.1.call-update) | async-done | bytes 327696 | tf_op jit(solution)/shard_map/reduce_scatter | solution.py:101
  378.3 1.1 fusion.29
  379.4 1.3 multiply_reduce_fusion.1
  380.8 1.4 multiply_convert_fusion.1
  382.5 45.7 %all_gather.28 = bf16[32,8,1280]{2,1,0:T(8,128)(2,1)S(1)} all-gather(bf16[1,8,1280]{2,1,0:T(8,128)(2,1)S(1)} %pad_maximum_fusion.1), channel_id=1, replica_groups=mesh['dp'=8,'tensor'=32] {'tensor'}, dimensions={0}, use_global_device_ids=true | all-gather | bytes 675840 | tf_op jit(solution)/shard_map/all_gather | solution.py:127
  428.6 2.3 fusion.22
  431.1 73.0 %pmax.7 = f32[64]{0:T(128)S(1)} all-reduce(f32[64]{0:T(128)S(1)} %pad_maximum_fusion.2), channel_id=1, replica_groups=mesh['dp'=8,'tensor'=32] {'dp','tensor'}, use_global_device_ids=true, to_apply=%region_17.18 | all-reduce | flops 64 | bytes 512 | tf_op jit(solution)/shard_map/pmax | solution.py:149
  (82 shorter events, 7.9 us)
Async XLA Ops:
  7.2 265.2 %copy-start = (bf16[640,1280]{1,0:T(8,128)(2,1)S(1)}, bf16[640,1280]{1,0:T(8,128)(2,1)}, u32[]{:S(2)}) copy-start(bf16[640,1280]{1,0:T(8,128)(2,1)} %param.26) | copy-start | bytes 4915204
  7.2 86.3 %all-gather.9.cloned.1.call-start = ((), (), s32[]{:S(2)}) async-start(), calls=%async_computation.3 | async-start | bytes 10813440 | tf_op jit(solution)/shard_map/all_gather | solution.py:55
  11.9 3.3 copy-start.9
  13.9 3.2 copy-start.10
  14.8 5.4 %copy-start.8 = (s32[1,128]{1,0:T(1,128)S(1)}, s32[1,128]{1,0:T(1,128)}, u32[]{:S(2)}) copy-start(s32[1,128]{1,0:T(1,128)} %param.16) | copy-start | bytes 1540
  17.1 167.4 %all-gather.11.cloned.1.call-start = ((), (), s32[]{:S(2)}) async-start(), calls=%async_computation.4 | async-start | bytes 2967552 | tf_op jit(solution)/shard_map/all_gather | solution.py:60
  66.9 50.4 %copy-start.5 = (pred[128,4096]{1,0:T(8,128)(4,1)}, pred[128,4096]{1,0:T(8,128)(4,1)S(1)}, u32[]{:S(2)}) copy-start(pred[128,4096]{1,0:T(8,128)(4,1)S(1)} %fusion.14) | copy-start | bytes 1572868
  103.1 163.8 %all-gather.7.cloned.1.call-start = ((), (), s32[]{:S(2)}) async-start(), calls=%async_computation.1 | async-start | bytes 2949120 | tf_op jit(solution)/shard_map/all_gather | solution.py:97
  138.6 25.4 %copy-start.4 = (bf16[640,1280]{1,0:T(8,128)(2,1)S(1)}, bf16[640,1280]{1,0:T(8,128)(2,1)}, u32[]{:S(2)}) copy-start(bf16[640,1280]{1,0:T(8,128)(2,1)} %param.20) | copy-start | bytes 4915204
  138.6 25.9 %copy-start.6 = (f32[1280]{0:T(1024)S(1)}, f32[1280]{0:T(1024)}, u32[]{:S(2)}) copy-start(f32[1280]{0:T(1024)} %param.21) | copy-start | bytes 15364
  164.0 1.0 copy-start.1
  164.5 102.4 %copy-start.11 = (bf16[1280,640]{1,0:T(8,128)(2,1)S(1)}, bf16[1280,640]{1,0:T(8,128)(2,1)}, u32[]{:S(2)}) copy-start(bf16[1280,640]{1,0:T(8,128)(2,1)} %param.22) | copy-start | bytes 4915204
  184.5 87.8 %copy-start.12 = (f32[640]{0:T(1024)S(1)}, f32[640]{0:T(1024)}, u32[]{:S(2)}) copy-start(f32[640]{0:T(1024)} %param.25) | copy-start | bytes 7684
  184.5 87.8 %copy-start.13 = (f32[640]{0:T(1024)S(1)}, f32[640]{0:T(1024)}, u32[]{:S(2)}) copy-start(f32[640]{0:T(1024)} %param.24) | copy-start | bytes 7684
  184.5 193.7 %reduce-scatter.2.cloned.1.call-start = ((), (), s32[]{:S(2)}) async-start(), calls=%async_computation.2 | async-start | bytes 2949120 | tf_op jit(solution)/shard_map/reduce_scatter | solution.py:101
  281.3 98.2 %copy-start.2 = (bf16[128,1280]{1,0:T(8,128)(2,1)S(1)}, bf16[128,1280]{1,0:T(8,128)(2,1)}, u32[]{:S(2)}) copy-start(bf16[128,1280]{1,0:T(8,128)(2,1)} %multiply_convert_fusion.2) | copy-start | bytes 983044
  281.3 98.2 %copy-start.7 = (f32[1280]{0:T(1024)S(1)}, f32[1280]{0:T(1024)}, u32[]{:S(2)}) copy-start(f32[1280]{0:T(1024)} %param.27) | copy-start | bytes 15364
  382.1 123.4 %copy-start.3 = (bf16[128,1280]{1,0:T(8,128)(2,1)}, bf16[128,1280]{1,0:T(8,128)(2,1)S(1)}, u32[]{:S(2)}) copy-start(bf16[128,1280]{1,0:T(8,128)(2,1)S(1)} %multiply_convert_fusion.1) | copy-start | bytes 983044
  382.1 122.0 %copy-start.14 = (s32[32]{0:T(128)S(1)}, s32[32]{0:T(128)}, u32[]{:S(2)}) copy-start(s32[32]{0:T(128)} %param.17) | copy-start | bytes 388
Sparse Core Ops, SparseCore 0:
  17.2 76.2 all-gather.8
  103.2 81.2 all-gather.10
  187.7 79.1 all-gather.6
  281.4 96.8 reduce-scatter.1
where the time goes:
time: 513 us; the launch traced here: 512 us
  waiting for transfers between devices  223 us (43%)
  blocking collectives  165 us (32%)
  matrix products  61.7 us (12%)
  other arithmetic  32.6 us (6%)
  local copies, waits for them, and re-layouts  15.6 us (3%)
  between operations  14.1 us (3%)
    reduce_scatter x1, waiting for transfers between devices, local(): lax.psum_scatter(jnp.dot(hidden, w_down, preferred_element_type=jnp.float...  95.8 us
    all_gather x1, waiting for transfers between devices, local(): received = lax.all_gather(mid_rows, 'dp', axis=0, tiled=True)  82.3 us
    pmax x1, blocking collectives, local(): lax.pmax(jnp.concatenate([spread_max, spread_norm]), ('dp', 'tensor'))  73 us
    all_gather x1, blocking collectives, local(): seg_all = lax.all_gather(segments, 'tensor', axis=0, tiled=True)  46.1 us
    all_gather x1, blocking collectives, local(): lax.all_gather(partial.astype(jnp.bfloat16), 'tensor', axis=0, tiled=False)  45.7 us
    all_gather x1, waiting for transfers between devices, local(): gathered = lax.all_gather(packed, 'tensor', axis=0, tiled=False)  26.5 us
    dot_general x1, matrix products, local(): jnp.dot(weights.astype(jnp.bfloat16).reshape(HEADS * row_count, total_key...  25.4 us
    sub x1, other arithmetic, local(): scores - row_max[:, :, None]  21.3 us
  transfers between devices with their start and end apart: 4, of which 4 were waited for; matrix products, arithmetic and copies ran while one was open for 13% of the time, Pallas kernels for 0%

commit v1 on v0

--- a/solution.py
+++ b/solution.py
@@ -94,7 +94,9 @@
     residual_in = start_rows.astype(jnp.float32)
     mid_rows = normalize(residual_in + alpha_attn * (attn_rows - residual_in)).astype(jnp.bfloat16)
     mid_rows, vocab_all = lax.optimization_barrier((mid_rows, vocab_all))
-    received = lax.all_gather(mid_rows, "dp", axis=0, tiled=True)
+    received = jnp.concatenate(
+        lax.all_to_all(jnp.stack(lax.axis_size("dp") * [mid_rows]), "dp", 0, 0), axis=0
+    )
     up_proj = jnp.dot(received, w_up, preferred_element_type=jnp.float32) * up_gain
     gate_proj = jnp.dot(received, w_gate, preferred_element_type=jnp.float32) * gate_gain
     hidden = (up_proj * jax.nn.silu(gate_proj)).astype(jnp.bfloat16)

time: 513 us -> 497 us (0.969)
  waiting for transfers between devices: 223 us -> 172 us
  blocking collectives: 165 us -> 201 us
    all_gather x1 -> x0, waiting for transfers between devices: 82.3 us -> none  [local(): received = lax.all_gather(mid_rows, 'dp', axis=0, tiled=True)]
    all_to_all x0 -> x1, blocking collectives: none -> 36.4 us  [local(): lax.all_to_all(jnp.stack(lax.axis_size('dp') * [mid_rows]), 'dp', 0, 0)]
    reduce_scatter x1, waiting for transfers between devices: 95.8 us -> 126 us  [local(): lax.psum_scatter(jnp.dot(hidden, w_down, preferred_element_type=jnp.float...]
  transfers between devices with their start and end apart: 4 -> 3, of which waited for: 4 -> 3; matrix products, arithmetic and copies ran while one was open for 13% -> 13% of each run, Pallas kernels for 0% -> 0%
where the time goes in v1:
time: 497 us; the launch traced here: 496 us
  blocking collectives  201 us (40%)
  waiting for transfers between devices  172 us (35%)
  matrix products  60 us (12%)
  other arithmetic  31.9 us (6%)
  local copies, waits for them, and re-layouts  17.3 us (3%)
  between operations  14 us (3%)
    reduce_scatter x1, waiting for transfers between devices, local(): lax.psum_scatter(jnp.dot(hidden, w_down, preferred_element_type=jnp.float...  126 us
    pmax x1, blocking collectives, local(): lax.pmax(jnp.concatenate([spread_max, spread_norm]), ('dp', 'tensor'))  73 us
    all_gather x1, blocking collectives, local(): seg_all = lax.all_gather(segments, 'tensor', axis=0, tiled=True)  46.1 us
    all_gather x1, blocking collectives, local(): lax.all_gather(partial.astype(jnp.bfloat16), 'tensor', axis=0, tiled=False)  45.6 us
    all_to_all x1, blocking collectives, local(): lax.all_to_all(jnp.stack(lax.axis_size('dp') * [mid_rows]), 'dp', 0, 0)  36.4 us
    all_gather x1, waiting for transfers between devices, local(): gathered = lax.all_gather(packed, 'tensor', axis=0, tiled=False)  26.5 us
    dot_general x1, matrix products, local(): jnp.dot(weights.astype(jnp.bfloat16).reshape(HEADS * row_count, total_key...  25.4 us
    sub x1, other arithmetic, local(): scores - row_max[:, :, None]  21.3 us
  transfers between devices with their start and end apart: 3, of which 3 were waited for; matrix products, arithmetic and copies ran while one was open for 13% of the time, Pallas kernels for 0%

profile of v1, /device:TPU:1, one launch (start us, length us, event | category | flops | bytes accessed | tf_op | source)
XLA Modules:
  0.0 496.5 jit_solution(5060930470565189501)
XLA Ops:
  7.2 1.2 fusion.30
  8.5 3.4 fusion.62
  12.9 1.0 reduce_sum.118
  13.9 0.9 copy.27
  15.3 1.0 multiply_convert_fusion.4
  17.2 3.1 concatenate.24
  20.3 46.1 %all-gather = s32[1,4096]{1,0:T(1,128)S(1)} all-gather(s32[1,128]{1,0:T(1,128)S(1)} %copy-done.8), channel_id=2, replica_groups=mesh['dp'=8,'tensor'=32] {'tensor'}, dimensions={1}, use_global_device_ids=true | all-gather | bytes 16896 | tf_op jit(solution)/shard_map/all_gather | solution.py:63
  66.9 26.5 %all-gather.6.cloned.1.call-done = bf16[4096,1280]{1,0:T(8,128)(2,1)} async-done(((bf16[128,1280]{1,0:T(8,128)(2,1)}), bf16[4096,1280]{1,0:T(8,128)(2,1)}) %all-gather.6.cloned.1.call-update) | async-done | bytes 10485776 | tf_op jit(solution)/shard_map/all_gather | solution.py:55
  93.5 9.6 %fusion.64 = (bf16[32,128,640]{2,1,0:T(8,128)(2,1)}, bf16[32,128,640]{2,1,0:T(8,128)(2,1)}) fusion(bf16[32,128,1280]{2,1,0:T(8,128)(2,1)} %bitcast.59), kind=kLoop, calls=%fused_computation.115 | loop fusion | bytes 20971520 | tf_op jit(solution)/shard_map/slice | solution.py:61
  103.3 13.9 %fusion.17 = f32[10,128,4096]{2,1,0:T(8,128)} fusion(bf16[4096,640,1]{1,0,2:T(8,128)(2,1)} %bitcast.61, bf16[10,640]{1,0:T(8,128)(2,1)S(1)} %get-tuple-element.17, bf16[128,640]{1,0:T(8,128)(2,1)S(1)} %get-tuple-element.13), kind=kOutput, calls=%fused_computation.21 | convolution fusion | flops 6711705600 | bytes 26391040 | tf_op jit(solution)/shard_map/dot_general | solution.py:76
  117.3 21.3 %fusion.65 = f32[10,128]{1,0:T(8,128)S(1)} fusion(f32[10,128,4096]{2,1,0:T(8,128)} %fusion.17, pred[128,4096]{1,0:T(8,128)(4,1)S(1)} %fusion.14), kind=kOutput, calls=%fused_computation.116 | output fusion | flops 31461376 | bytes 21500928 | tf_op jit(solution)/shard_map/sub | solution.py:83
  138.6 25.4 %multiply_reduce_fusion = bf16[128,640]{1,0:T(8,128)(2,1)S(1)} fusion(bf16[4096,640,1]{1,0,2:T(8,128)(2,1)} %bitcast.60, f32[10,640]{1,0:T(8,128)S(1)} %get-tuple-element.18, f32[10,128]{1,0:T(8,128)S(1)} %fusion.65, f32[10,128,4096]{2,1,0:T(8,128)} %fusion.17, pred[128,4096]{1,0:T(8,128)(4,1)} %copy-done.5), kind=kOutput, calls=%fused_computation.11 | convolution fusion | flops 6744724480 | bytes 26933248 | tf_op jit(solution)/shard_map/dot_general | solution.py:85
  165.6 18.9 %all-gather.8.cloned.1.call-done = bf16[10304,125]{1,0:T(8,128)(2,1)} async-done(((bf16[1288,125]{1,0:T(8,128)(2,1)}), bf16[10304,125]{1,0:T(8,128)(2,1)}) %all-gather.8.cloned.1.call-update) | async-done | bytes 2576016 | tf_op jit(solution)/shard_map/all_gather | solution.py:60
  184.7 36.4 %all_to_all.5 = bf16[8,128,1280]{2,1,0:T(8,128)(2,1)S(1)} all-to-all(bf16[8,128,1280]{2,1,0:T(8,128)(2,1)S(1)} %stack.2), channel_id=1, replica_groups=mesh['dp'=8,'tensor'=32] {'dp'}, dimensions={0} | all-to-all | bytes 5242880 | tf_op jit(solution)/shard_map/all_to_all | solution.py:98
  221.1 1.5 copy-done.3
  222.6 3.7 fusion.66
  226.4 8.9 %convolution_convert_fusion = bf16[1024,1280]{1,0:T(8,128)(2,1)} fusion(bf16[640,1280]{1,0:T(8,128)(2,1)S(1)} %copy-done, f32[1024,640]{1,0:T(8,128)} %fusion.66, bf16[1024,1280]{1,0:T(8,128)(2,1)} %bitcast.64, bf16[1280,640]{1,0:T(8,128)(2,1)} %param.23, f32[640]{0:T(1024)S(1)} %copy-done.12, f32[640]{0:T(1024)S(1)} %copy-done.13), kind=kOutput, calls=%fused_computation.10 | convolution fusion | flops 3361996800 | bytes 11146240 | tf_op jit(solution)/shard_map/dot_general | solution.py:104
  236.5 126.3 %reduce-scatter.2.cloned.1.call-done = bf16[128,1280]{1,0:T(8,128)(2,1)} async-done(((bf16[1024,1280]{1,0:T(8,128)(2,1)}), bf16[128,1280]{1,0:T(8,128)(2,1)}) %reduce-scatter.2.cloned.1.call-update) | async-done | bytes 327696 | tf_op jit(solution)/shard_map/reduce_scatter | solution.py:103
  362.8 1.1 fusion.29
  363.9 1.3 multiply_reduce_fusion.1
  365.2 1.4 multiply_convert_fusion.1
  367.0 45.6 %all_gather.24 = bf16[32,8,1280]{2,1,0:T(8,128)(2,1)S(1)} all-gather(bf16[1,8,1280]{2,1,0:T(8,128)(2,1)S(1)} %pad_maximum_fusion.1), channel_id=1, replica_groups=mesh['dp'=8,'tensor'=32] {'tensor'}, dimensions={0}, use_global_device_ids=true | all-gather | bytes 675840 | tf_op jit(solution)/shard_map/all_gather | solution.py:129
  413.0 2.3 fusion.22
  415.5 73.0 %pmax.7 = f32[64]{0:T(128)S(1)} all-reduce(f32[64]{0:T(128)S(1)} %pad_maximum_fusion.2), channel_id=1, replica_groups=mesh['dp'=8,'tensor'=32] {'dp','tensor'}, use_global_device_ids=true, to_apply=%region_17.18 | all-reduce | flops 64 | bytes 512 | tf_op jit(solution)/shard_map/pmax | solution.py:151
  (81 shorter events, 8.3 us)
Async XLA Ops:
  7.2 219.2 %copy-start = (bf16[640,1280]{1,0:T(8,128)(2,1)S(1)}, bf16[640,1280]{1,0:T(8,128)(2,1)}, u32[]{:S(2)}) copy-start(bf16[640,1280]{1,0:T(8,128)(2,1)} %param.26) | copy-start | bytes 4915204
  7.2 86.3 %all-gather.6.cloned.1.call-start = ((), (), s32[]{:S(2)}) async-start(), calls=%async_computation.3 | async-start | bytes 10813440 | tf_op jit(solution)/shard_map/all_gather | solution.py:55
  11.9 3.3 copy-start.9
  13.9 3.2 copy-start.10
  14.8 5.4 %copy-start.8 = (s32[1,128]{1,0:T(1,128)S(1)}, s32[1,128]{1,0:T(1,128)}, u32[]{:S(2)}) copy-start(s32[1,128]{1,0:T(1,128)} %param.16) | copy-start | bytes 1540
  17.1 167.4 %all-gather.8.cloned.1.call-start = ((), (), s32[]{:S(2)}) async-start(), calls=%async_computation.4 | async-start | bytes 2967552 | tf_op jit(solution)/shard_map/all_gather | solution.py:60
  66.9 50.4 %copy-start.5 = (pred[128,4096]{1,0:T(8,128)(4,1)}, pred[128,4096]{1,0:T(8,128)(4,1)S(1)}, u32[]{:S(2)}) copy-start(pred[128,4096]{1,0:T(8,128)(4,1)S(1)} %fusion.14) | copy-start | bytes 1572868
  103.1 259.7 %reduce-scatter.2.cloned.1.call-start = ((), (), s32[]{:S(2)}) async-start(), calls=%async_computation.2 | async-start | bytes 2949120 | tf_op jit(solution)/shard_map/reduce_scatter | solution.py:103
  138.6 25.4 %copy-start.4 = (bf16[640,1280]{1,0:T(8,128)(2,1)S(1)}, bf16[640,1280]{1,0:T(8,128)(2,1)}, u32[]{:S(2)}) copy-start(bf16[640,1280]{1,0:T(8,128)(2,1)} %param.20) | copy-start | bytes 4915204
  138.6 25.9 %copy-start.6 = (f32[1280]{0:T(1024)S(1)}, f32[1280]{0:T(1024)}, u32[]{:S(2)}) copy-start(f32[1280]{0:T(1024)} %param.21) | copy-start | bytes 15364
  164.0 1.0 copy-start.1
  184.7 37.9 %copy-start.11 = (bf16[1280,640]{1,0:T(8,128)(2,1)S(1)}, bf16[1280,640]{1,0:T(8,128)(2,1)}, u32[]{:S(2)}) copy-start(bf16[1280,640]{1,0:T(8,128)(2,1)} %param.22) | copy-start | bytes 4915204
  221.1 1.5 copy-start.3
  222.6 3.8 copy-start.12
  222.6 3.8 copy-start.13
  235.3 128.6 %copy-start.7 = (f32[1280]{0:T(1024)S(1)}, f32[1280]{0:T(1024)}, u32[]{:S(2)}) copy-start(f32[1280]{0:T(1024)} %param.27) | copy-start | bytes 15364
  366.6 123.4 %copy-start.2 = (bf16[128,1280]{1,0:T(8,128)(2,1)}, bf16[128,1280]{1,0:T(8,128)(2,1)S(1)}, u32[]{:S(2)}) copy-start(bf16[128,1280]{1,0:T(8,128)(2,1)S(1)} %multiply_convert_fusion.1) | copy-start | bytes 983044
  366.6 121.9 %copy-start.14 = (s32[32]{0:T(128)S(1)}, s32[32]{0:T(128)}, u32[]{:S(2)}) copy-start(s32[32]{0:T(128)} %param.17) | copy-start | bytes 388
Sparse Core Ops, SparseCore 0:
  17.2 76.2 all-gather.5
  103.2 81.2 all-gather.7
  235.4 127.2 reduce-scatter.1
